TPU v7x, 32 devices: a whole 2x2x4 slice. The times are simulated.
32 devices in a mesh: year: 8 (over z, x), region: 4 (over y, core).
Axes of the slice: x: 2, y: 2, z: 4, core: 2. Of those that a mesh axis runs over, the one named last changes fastest.
Arguments:
- daily_temps: bfloat16 [8, 22, 512], P('year', None, 'region'), may hold values from -6 to 6
- land_mask: int32 [512], P('region'), may hold values 0 or 1
Outputs:
- coarse_threshold: float32 [8, 512], P('year', 'region')
- refined_threshold: float32 [8, 512], P('year', 'region')
All inputs are finite; a program needn't handle non-finite values. No bound on the sum of `land_mask` on one device may be relied on, other than what follows from the above.
Results may differ from a plain program's by a relative error of at most 0.0013.
Values may be sent and summed in bfloat16 or wider, within the bound.
No kernel may reach another device: no remote copies, remote signals or barrier semaphores. Data moves between devices by JAX's collectives and lax.ppermute only.
A program may use at most 64 MiB of HBM per device.

v0:
```python
import jax
import jax.numpy as jnp
from jax import lax
from jax.sharding import PartitionSpec as P

WIN = 15
BINS = 256
VALUE_RANGE = 12.8
QUANT_LEVEL = 0.9
SHARPNESS = 32.0
KERNEL_SCALE = 0.25
STEP_SIZE = 2.0


def extended_2(array, sides, width):
    for axis, dim in sides:
        devices, length = (lax.axis_size(axis), array.shape[dim])
        up = [(i, (i + 1) % devices) for i in range(devices)]
        down = [(j, i) for i, j in up]
        last = lax.slice_in_dim(array, length - width, length, axis=dim)
        leading = lax.slice_in_dim(array, 0, width, axis=dim)
        before = lax.ppermute(last, axis, up)
        after = lax.ppermute(leading, axis, down)
        array = jnp.concatenate([before, array, after], axis=dim)
    return array


def smooth_field(extended, flags):
    center = extended[..., 1:-1]
    same_west = 1.0 - jnp.abs(flags[1:-1] - flags[:-2])
    same_east = 1.0 - jnp.abs(flags[1:-1] - flags[2:])
    mixed = center + same_west * extended[..., :-2] + same_east * extended[..., 2:]
    return (mixed / (1.0 + same_west + same_east)).astype(jnp.bfloat16)


def bin_weights(year_field, bin_count):
    width = VALUE_RANGE / bin_count
    scaled = jnp.clip(
        (year_field.astype(jnp.float32) + 0.5 * VALUE_RANGE) / width, 0.0, bin_count - 1.0
    )
    centers = jnp.arange(bin_count, dtype=jnp.float32)
    return jnp.maximum(0.0, 1.0 - jnp.abs(scaled[..., None] - centers)).astype(jnp.bfloat16)


def quantile(histogram, count_all, bin_count):
    width = VALUE_RANGE / bin_count
    cumulative = jnp.cumsum(histogram, axis=-1)
    ranks = jnp.clip(0.5 + SHARPNESS * (QUANT_LEVEL - cumulative / count_all), 0.0, 1.0)
    return -0.5 * VALUE_RANGE + width * jnp.sum(ranks, axis=-1)


def day_band(row_count, days_in):
    row_day = lax.broadcasted_iota(jnp.int32, (row_count, days_in), 0)
    column_day = lax.broadcasted_iota(jnp.int32, (row_count, days_in), 1)
    inside = (column_day >= row_day) & (column_day < row_day + WIN)
    return jnp.where(inside, 1.0, 0.0).astype(jnp.bfloat16)


def window_cdf(threshold, year_field):
    cal_days = threshold.shape[0]
    samples = year_field.astype(jnp.float32)
    running = jnp.zeros(threshold.shape, jnp.float32)
    for offset in range(WIN):
        window = samples[:, offset : offset + cal_days, :]
        running = running + jnp.sum(
            jax.nn.sigmoid((threshold[None] - window) / KERNEL_SCALE), axis=0
        )
    return running


def shards(daily_temps, land_mask):
    days_in = daily_temps.shape[1]
    lon_cells = daily_temps.shape[2]
    year_count = lax.axis_size("year")
    cal_days = days_in - WIN + 1
    cal_own = cal_days // year_count
    count_all = float(year_count * WIN)
    flag_row = land_mask.astype(jnp.bfloat16)[None, :]
    stacked = jnp.concatenate([daily_temps[0], flag_row], axis=0)
    extended = extended_2(stacked, (("region", 1),), 1)
    smoothed = smooth_field(
        extended[:days_in].astype(jnp.float32), extended[days_in].astype(jnp.float32)
    )
    weights = bin_weights(smoothed, BINS).reshape(days_in, lon_cells * BINS)
    own_rows = lax.psum_scatter(
        jnp.dot(
            day_band(cal_own * lax.axis_size("year"), days_in),
            weights,
            preferred_element_type=jnp.float32,
        ),
        "year",
        scatter_dimension=0,
        tiled=True,
    )
    coarse = quantile(own_rows.reshape(cal_own, lon_cells, BINS), count_all, BINS)
    coarse_all = lax.all_gather(coarse, "year", axis=0, tiled=True)
    partial_cdf = window_cdf(coarse_all, smoothed[None])
    cdf_whole = lax.psum(partial_cdf, "year")
    own_cdf = lax.dynamic_slice_in_dim(cdf_whole, lax.axis_index("year") * cal_own, cal_own, 0)
    refined = coarse - STEP_SIZE * (own_cdf / count_all - QUANT_LEVEL)
    return (coarse, refined)


def solution(mesh):
    return jax.shard_map(
        shards,
        mesh=mesh,
        in_specs=(P("year", None, "region"), P("region")),
        out_specs=(P("year", "region"), P("year", "region")),
        check_vma=False,
    )
```

profile of v0, /device:TPU:0, one launch (start us, length us, event | category | flops | bytes accessed | tf_op | source)
XLA Modules:
  0.0 145.1 jit_solution(3068982300265254493)
XLA Ops:
  7.2 0.0 all-reduce.3.cloned.1.call-start
  7.2 0.7 convert_bitcast_fusion.1
  7.9 0.8 slice_maximum_fusion
  8.7 2.4 %collective-permute-start.1 = (bf16[23,1]{1,0:T(8,128)(2,1)S(1)}, bf16[23,1]{1,0:T(8,128)(2,1)S(1)}, u32[]{:S(2)}, u32[]{:S(2)}) collective-permute-start(bf16[23,1]{1,0:T(8,128)(2,1)S(1)} %get-tuple-element.9), channel_id=1, source_target_pairs={{1,0},{2,1},{3,2},{0,3},{5,4},{6,5},{7,6},{4,7},{9,8},{10,9},{11,1... | collective-permute-start | bytes 146 | tf_op jit(solution)/shard_map/ppermute | solution.py:23
  11.1 0.0 collective-permute-start
  11.2 0.1 copy.8
  11.2 1.2 collective-permute-done.1
  12.5 1.7 %collective-permute-done = bf16[23,1]{1,0:T(8,128)(2,1)S(1)} collective-permute-done((bf16[23,1]{1,0:T(8,128)(2,1)S(1)}, bf16[23,1]{1,0:T(8,128)(2,1)S(1)}, u32[]{:S(2)}, u32[]{:S(2)}) %collective-permute-start) | collective-permute-done | bytes 78 | tf_op jit(solution)/shard_map/ppermute | solution.py:22
  14.2 0.8 maximum_convert_fusion.2
  14.9 0.1 bitcast_add_fusion
  15.0 0.1 subtract_bitcast_fusion.1
  15.1 0.8 pad_maximum_fusion
  15.9 0.1 convert_bitcast_fusion
  16.0 0.4 sub.122
  16.4 0.3 pad.12
  16.8 1.8 %copy.7 = f32[3,8,128,256]{3,1,2,0:T(8,128)S(1)} copy(f32[3,8,128,256]{3,2,1,0:T(8,128)S(1)} %bitcast.36) | data formatting | bytes 6291456
  18.6 0.0 copy-start
  18.6 1.8 %fusion = f32[8,32768]{1,0:T(8,128)} fusion(f32[22,32768]{1,0:T(8,128)S(1)} %bitcast.35, f32[32768]{0:T(1024)S(1)} %bitcast.37, s32[8]{0:T(128)S(1)} %iota_add_fusion), kind=kOutput, calls=%fused_computation.1 | convolution fusion | flops 15139696 | bytes 4063264 | tf_op jit(solution)/shard_map/dot_general | solution.py:86
  20.4 0.0 all-reduce.3.cloned.1.call-update
  20.5 0.0 copy-done
  20.5 0.6 dynamic-slice
  21.1 77.9 %all-reduce.3.cloned.1.call-done = f32[8,32768]{1,0:T(8,128)} async-done(((f32[8,32768]{1,0:T(8,128)}), f32[8,32768]{1,0:T(8,128)}) %all-reduce.3.cloned.1.call-update) | async-done | bytes 1048592
  99.0 2.0 %constant_dynamic-slice_fusion = f32[1,32768]{1,0:T(1,128)S(1)} fusion(f32[8,32768]{1,0:T(8,128)} %all-reduce.3.cloned.1.call-done, u32[]{:T(128)} %bitcast.13), kind=kLoop, calls=%fused_computation.140 | loop fusion | bytes 262148
  101.0 0.1 copy.6
  101.1 0.1 fusion.112
  101.3 0.2 clamp_reduce_fusion
  101.4 19.1 %all-gather.1 = f32[8,1,128]{2,1,0:T(1,128)S(1)} all-gather(f32[1,1,128]{2,1,0:T(1,128)S(1)} %fusion.106), channel_id=2, replica_groups=mesh['year'=8,'region'=4] {'year'}, dimensions={0}, use_global_device_ids=true | all-gather | bytes 4608 | tf_op jit(solution)/shard_map/all_gather | solution.py:96
  120.5 17.1 %psum.7 = f32[8,128]{1,0:T(8,128)S(1)} all-reduce(f32[8,128]{1,0:T(8,128)S(1)} %fusion.16), channel_id=1, replica_groups=mesh['year'=8,'region'=4] {'year'}, use_global_device_ids=true, to_apply=%region_4.5 | all-reduce | flops 1024 | bytes 8192 | tf_op jit(solution)/shard_map/psum | solution.py:98
  137.7 0.5 multiply_subtract_fusion
  (9 shorter events, 0.1 us)
Async XLA Ops:
  7.2 91.8 %all-reduce.3.cloned.1.call-start = ((), (), s32[]{:S(2)}) async-start(), calls=%async_computation | async-start | bytes 2097152
  8.7 3.8 %collective-permute-start.1 = (bf16[23,1]{1,0:T(8,128)(2,1)S(1)}, bf16[23,1]{1,0:T(8,128)(2,1)S(1)}, u32[]{:S(2)}, u32[]{:S(2)}) collective-permute-start(bf16[23,1]{1,0:T(8,128)(2,1)S(1)} %get-tuple-element.9), channel_id=1, source_target_pairs={{1,0},{2,1},{3,2},{0,3},{5,4},{6,5},{7,6},{4,7},{9,8},{10,9},{11,1... | collective-permute-start | bytes 146 | tf_op jit(solution)/shard_map/ppermute | solution.py:23
  11.1 3.1 %collective-permute-start = (bf16[23,1]{1,0:T(8,128)(2,1)S(1)}, bf16[23,1]{1,0:T(8,128)(2,1)S(1)}, u32[]{:S(2)}, u32[]{:S(2)}) collective-permute-start(bf16[23,1]{1,0:T(8,128)(2,1)S(1)} %get-tuple-element.8), channel_id=1, source_target_pairs={{0,1},{1,2},{2,3},{3,0},{4,5},{5,6},{6,7},{7,4},{8,9},{9,10},{10,1... | collective-permute-start | bytes 146 | tf_op jit(solution)/shard_map/ppermute | solution.py:22
  18.6 1.9 %copy-start = (u32[32]{0:T(128)S(1)}, u32[32]{0:T(128)}, u32[]{:S(2)}) copy-start(u32[32]{0:T(128)} %constant.71) | copy-start | bytes 388
Sparse Core Ops, SparseCore 0:
  20.6 78.3 all-reduce.2
where the time goes:
time: 145 us
  waiting for transfers between devices  80.9 us (56%)
  blocking collectives  36.2 us (25%)
  between operations  14.1 us (10%)
  local copies, waits for them, and re-layouts  5.36 us (4%)
  other arithmetic  4.19 us (3%)
  starting transfers between devices  2.45 us (2%)
  matrix products  1.83 us (1%)
    unnamed x2, waiting for transfers between devices  78 us
    all_gather x1, blocking collectives, shards(): coarse_all = lax.all_gather(coarse, 'year', axis=0, tiled=True)  19.1 us
    psum x1, blocking collectives, shards(): cdf_whole = lax.psum(partial_cdf, 'year')  17.1 us
    unnamed x8, local copies, waits for them, and re-layouts  4.8 us
  transfers between devices with their start and end apart: 3, of which 3 were waited for; matrix products, arithmetic and copies ran while one was open for 0% of the time, Pallas kernels for 0%

commit v1 on v0

--- a/solution.py
+++ b/solution.py
@@ -10,6 +10,22 @@
 SHARPNESS = 32.0
 KERNEL_SCALE = 0.25
 STEP_SIZE = 2.0
+
+
+def connect_flows(out_dim, chip_axis, x_local):
+    q_n = jax.lax.axis_size(chip_axis)
+    oldest = x_local
+    history = [oldest]
+    placed = sorted(((h, (h + 1) % q_n) for h in range(q_n)))
+    for no in [*range(1, q_n)]:
+        oldest = jax.lax.ppermute(oldest, chip_axis, placed)
+        history.insert(0, oldest)
+    part_now = jnp.roll(
+        jnp.concatenate(history, axis=out_dim),
+        shift=(jax.lax.axis_index(chip_axis) + 1) * x_local.shape[out_dim],
+        axis=out_dim,
+    )
+    return part_now
 
 
 def extended_2(array, sides, width):
@@ -93,7 +109,7 @@
         tiled=True,
     )
     coarse = quantile(own_rows.reshape(cal_own, lon_cells, BINS), count_all, BINS)
-    coarse_all = lax.all_gather(coarse, "year", axis=0, tiled=True)
+    coarse_all = connect_flows(0, "year", x_local=coarse)
     partial_cdf = window_cdf(coarse_all, smoothed[None])
     cdf_whole = lax.psum(partial_cdf, "year")
     own_cdf = lax.dynamic_slice_in_dim(cdf_whole, lax.axis_index("year") * cal_own, cal_own, 0)

time: 145 us -> 170 us (1.17)
  waiting for transfers between devices: 80.9 us -> 124 us
  blocking collectives: 36.2 us -> 17.1 us
    ppermute x0 -> x7, waiting for transfers between devices: none -> 42.4 us  [connect_flows(): oldest = jax.lax.ppermute(oldest, chip_axis, placed)]
    all_gather x1 -> x0, blocking collectives: 19.1 us -> none  [shards(): coarse_all = lax.all_gather(coarse, 'year', axis=0, tiled=True)]
    unnamed x2, waiting for transfers between devices: 78 us -> 80 us
    unnamed x8 -> x10, local copies, waits for them, and re-layouts: 4.8 us -> 4.8 us
  transfers between devices with their start and end apart: 3 -> 10, of which waited for: 3 -> 10; matrix products, arithmetic and copies ran while one was open for 0% -> 0% of each run, Pallas kernels for 0% -> 0%
where the time goes in v1:
time: 170 us
  waiting for transfers between devices  124 us (73%)
  blocking collectives  17.1 us (10%)
  between operations  14.1 us (8%)
  local copies, waits for them, and re-layouts  5.41 us (3%)
  other arithmetic  4.19 us (2%)
  starting transfers between devices  3.82 us (2%)
  matrix products  1.82 us (1%)
    unnamed x2, waiting for transfers between devices  80 us
    ppermute x7, waiting for transfers between devices, connect_flows(): oldest = jax.lax.ppermute(oldest, chip_axis, placed)  42.4 us
    psum x1, blocking collectives, shards(): cdf_whole = lax.psum(partial_cdf, 'year')  17.1 us
    unnamed x10, local copies, waits for them, and re-layouts  4.8 us
  transfers between devices with their start and end apart: 10, of which 10 were waited for; matrix products, arithmetic and copies ran while one was open for 0% of the time, Pallas kernels for 0%

profile of v1, /device:TPU:0, one launch (start us, length us, event | category | flops | bytes accessed | tf_op | source)
XLA Modules:
  0.0 170.1 jit_solution(14202258594101671444)
XLA Ops:
  7.2 0.7 convert_bitcast_fusion.1
  7.9 0.8 slice_maximum_fusion
  8.7 0.5 collective-permute-start
  9.2 2.0 %collective-permute-start.1 = (bf16[23,1]{1,0:T(8,128)(2,1)S(1)}, bf16[23,1]{1,0:T(8,128)(2,1)S(1)}, u32[]{:S(2)}, u32[]{:S(2)}) collective-permute-start(bf16[23,1]{1,0:T(8,128)(2,1)S(1)} %get-tuple-element.7), channel_id=1, source_target_pairs={{1,0},{2,1},{3,2},{0,3},{5,4},{6,5},{7,6},{4,7},{9,8},{10,9},{11,1... | collective-permute-start | bytes 146 | tf_op jit(solution)/shard_map/ppermute | solution.py:39
  11.2 0.1 copy.7
  11.3 1.2 collective-permute-done
  12.4 0.1 collective-permute-done.1
  12.5 0.8 maximum_convert_fusion.2
  13.3 0.1 bitcast_add_fusion
  13.4 0.1 subtract_bitcast_fusion.1
  13.4 0.8 pad_maximum_fusion
  14.2 0.1 convert_bitcast_fusion
  14.3 0.4 sub.126
  14.8 0.3 pad.12
  15.1 1.8 %copy.6 = f32[3,8,128,256]{3,1,2,0:T(8,128)S(1)} copy(f32[3,8,128,256]{3,2,1,0:T(8,128)S(1)} %bitcast.34) | data formatting | bytes 6291456
  16.9 1.8 %fusion = f32[8,32768]{1,0:T(8,128)} fusion(f32[22,32768]{1,0:T(8,128)S(1)} %bitcast.33, f32[32768]{0:T(1024)S(1)} %bitcast.35, s32[8]{0:T(128)S(1)} %iota_add_fusion), kind=kOutput, calls=%fused_computation.1 | convolution fusion | flops 15139696 | bytes 4063264 | tf_op jit(solution)/shard_map/dot_general | solution.py:102
  18.8 0.6 dynamic-slice
  19.4 79.9 %all-reduce.3.cloned.1.call-done = f32[8,32768]{1,0:T(8,128)} async-done(((f32[8,32768]{1,0:T(8,128)}), f32[8,32768]{1,0:T(8,128)}) %all-reduce.3.cloned.1.call-update) | async-done | bytes 1048592
  99.3 2.0 %constant_dynamic-slice_fusion = f32[1,32768]{1,0:T(1,128)S(1)} fusion(f32[8,32768]{1,0:T(8,128)} %all-reduce.3.cloned.1.call-done, u32[]{:T(128)} %bitcast.12), kind=kLoop, calls=%fused_computation.140 | loop fusion | bytes 262148
  101.3 0.1 copy.5
  101.4 0.1 fusion.109
  101.6 0.2 clamp_reduce_fusion
  101.8 1.3 collective-permute-start.2
  103.1 5.0 %collective-permute-done.2 = f32[1,128]{1,0:T(1,128)S(1)} collective-permute-done((f32[1,128]{1,0:T(1,128)S(1)}, f32[1,128]{1,0:T(1,128)S(1)}, u32[]{:S(2)}, u32[]{:S(2)}) %collective-permute-start.2) | collective-permute-done | bytes 544 | tf_op jit(solution)/shard_map/ppermute | solution.py:21
  108.1 6.2 %collective-permute-done.3 = f32[1,128]{1,0:T(1,128)S(1)} collective-permute-done((f32[1,128]{1,0:T(1,128)S(1)}, f32[1,128]{1,0:T(1,128)S(1)}, u32[]{:S(2)}, u32[]{:S(2)}) %collective-permute-start.3) | collective-permute-done | bytes 544 | tf_op jit(solution)/shard_map/ppermute | solution.py:21
  114.3 6.2 %collective-permute-done.4 = f32[1,128]{1,0:T(1,128)S(1)} collective-permute-done((f32[1,128]{1,0:T(1,128)S(1)}, f32[1,128]{1,0:T(1,128)S(1)}, u32[]{:S(2)}, u32[]{:S(2)}) %collective-permute-start.4) | collective-permute-done | bytes 544 | tf_op jit(solution)/shard_map/ppermute | solution.py:21
  120.6 6.2 %collective-permute-done.5 = f32[1,128]{1,0:T(1,128)S(1)} collective-permute-done((f32[1,128]{1,0:T(1,128)S(1)}, f32[1,128]{1,0:T(1,128)S(1)}, u32[]{:S(2)}, u32[]{:S(2)}) %collective-permute-start.5) | collective-permute-done | bytes 544 | tf_op jit(solution)/shard_map/ppermute | solution.py:21
  126.8 6.2 %collective-permute-done.6 = f32[1,128]{1,0:T(1,128)S(1)} collective-permute-done((f32[1,128]{1,0:T(1,128)S(1)}, f32[1,128]{1,0:T(1,128)S(1)}, u32[]{:S(2)}, u32[]{:S(2)}) %collective-permute-start.6) | collective-permute-done | bytes 544 | tf_op jit(solution)/shard_map/ppermute | solution.py:21
  133.0 6.2 %collective-permute-done.7 = f32[1,128]{1,0:T(1,128)S(1)} collective-permute-done((f32[1,128]{1,0:T(1,128)S(1)}, f32[1,128]{1,0:T(1,128)S(1)}, u32[]{:S(2)}, u32[]{:S(2)}) %collective-permute-start.7) | collective-permute-done | bytes 544 | tf_op jit(solution)/shard_map/ppermute | solution.py:21
  139.3 6.2 %collective-permute-done.8 = f32[1,128]{1,0:T(1,128)S(1)} collective-permute-done((f32[1,128]{1,0:T(1,128)S(1)}, f32[1,128]{1,0:T(1,128)S(1)}, u32[]{:S(2)}, u32[]{:S(2)}) %collective-permute-start.8) | collective-permute-done | bytes 544 | tf_op jit(solution)/shard_map/ppermute | solution.py:21
  145.6 17.1 %psum.7 = f32[8,128]{1,0:T(8,128)S(1)} all-reduce(f32[8,128]{1,0:T(8,128)S(1)} %fusion.16), channel_id=1, replica_groups=mesh['year'=8,'region'=4] {'year'}, use_global_device_ids=true, to_apply=%region_4.5 | all-reduce | flops 1024 | bytes 8192 | tf_op jit(solution)/shard_map/psum | solution.py:114
  162.7 0.5 multiply_subtract_fusion
  (22 shorter events, 0.3 us)
Async XLA Ops:
  7.2 92.2 %all-reduce.3.cloned.1.call-start = ((), (), s32[]{:S(2)}) async-start(), calls=%async_computation | async-start | bytes 2097152
  8.7 3.7 %collective-permute-start = (bf16[23,1]{1,0:T(8,128)(2,1)S(1)}, bf16[23,1]{1,0:T(8,128)(2,1)S(1)}, u32[]{:S(2)}, u32[]{:S(2)}) collective-permute-start(bf16[23,1]{1,0:T(8,128)(2,1)S(1)} %get-tuple-element.6), channel_id=1, source_target_pairs={{0,1},{1,2},{2,3},{3,0},{4,5},{5,6},{6,7},{7,4},{8,9},{9,10},{10,1... | collective-permute-start | bytes 146 | tf_op jit(solution)/shard_map/ppermute | solution.py:38
  9.2 3.4 %collective-permute-start.1 = (bf16[23,1]{1,0:T(8,128)(2,1)S(1)}, bf16[23,1]{1,0:T(8,128)(2,1)S(1)}, u32[]{:S(2)}, u32[]{:S(2)}) collective-permute-start(bf16[23,1]{1,0:T(8,128)(2,1)S(1)} %get-tuple-element.7), channel_id=1, source_target_pairs={{1,0},{2,1},{3,2},{0,3},{5,4},{6,5},{7,6},{4,7},{9,8},{10,9},{11,1... | collective-permute-start | bytes 146 | tf_op jit(solution)/shard_map/ppermute | solution.py:39
  16.9 1.9 %copy-start.1 = (u32[32]{0:T(128)S(1)}, u32[32]{0:T(128)}, u32[]{:S(2)}) copy-start(u32[32]{0:T(128)} %constant.93) | copy-start | bytes 388
  101.8 61.5 %copy-start = (f32[1,128]{1,0:T(1,128)}, f32[1,128]{1,0:T(1,128)S(1)}, u32[]{:S(2)}) copy-start(f32[1,128]{1,0:T(1,128)S(1)} %add_bitcast_fusion) | copy-start | bytes 1540
  101.8 6.3 %collective-permute-start.2 = (f32[1,128]{1,0:T(1,128)S(1)}, f32[1,128]{1,0:T(1,128)S(1)}, u32[]{:S(2)}, u32[]{:S(2)}) collective-permute-start(f32[1,128]{1,0:T(1,128)S(1)} %add_bitcast_fusion), channel_id=1, source_target_pairs={{0,4},{4,8},{8,12},{12,16},{16,20},{20,24},{24,28},{28,0},{1,5},{5... | collective-permute-start | bytes 1544 | tf_op jit(solution)/shard_map/ppermute | solution.py:21
  108.1 6.2 %collective-permute-start.3 = (f32[1,128]{1,0:T(1,128)S(1)}, f32[1,128]{1,0:T(1,128)S(1)}, u32[]{:S(2)}, u32[]{:S(2)}) collective-permute-start(f32[1,128]{1,0:T(1,128)S(1)} %collective-permute-done.2), channel_id=1, source_target_pairs={{0,4},{4,8},{8,12},{12,16},{16,20},{20,24},{24,28},{28,0},{1,5},{5... | collective-permute-start | bytes 1544 | tf_op jit(solution)/shard_map/ppermute | solution.py:21
  114.3 6.2 %collective-permute-start.4 = (f32[1,128]{1,0:T(1,128)S(1)}, f32[1,128]{1,0:T(1,128)S(1)}, u32[]{:S(2)}, u32[]{:S(2)}) collective-permute-start(f32[1,128]{1,0:T(1,128)S(1)} %collective-permute-done.3), channel_id=1, source_target_pairs={{0,4},{4,8},{8,12},{12,16},{16,20},{20,24},{24,28},{28,0},{1,5},{5... | collective-permute-start | bytes 1544 | tf_op jit(solution)/shard_map/ppermute | solution.py:21
  120.5 6.2 %collective-permute-start.5 = (f32[1,128]{1,0:T(1,128)S(1)}, f32[1,128]{1,0:T(1,128)S(1)}, u32[]{:S(2)}, u32[]{:S(2)}) collective-permute-start(f32[1,128]{1,0:T(1,128)S(1)} %collective-permute-done.4), channel_id=1, source_target_pairs={{0,4},{4,8},{8,12},{12,16},{16,20},{20,24},{24,28},{28,0},{1,5},{5... | collective-permute-start | bytes 1544 | tf_op jit(solution)/shard_map/ppermute | solution.py:21
  126.8 6.2 %collective-permute-start.6 = (f32[1,128]{1,0:T(1,128)S(1)}, f32[1,128]{1,0:T(1,128)S(1)}, u32[]{:S(2)}, u32[]{:S(2)}) collective-permute-start(f32[1,128]{1,0:T(1,128)S(1)} %collective-permute-done.5), channel_id=1, source_target_pairs={{0,4},{4,8},{8,12},{12,16},{16,20},{20,24},{24,28},{28,0},{1,5},{5... | collective-permute-start | bytes 1544 | tf_op jit(solution)/shard_map/ppermute | solution.py:21
  133.0 6.2 %collective-permute-start.7 = (f32[1,128]{1,0:T(1,128)S(1)}, f32[1,128]{1,0:T(1,128)S(1)}, u32[]{:S(2)}, u32[]{:S(2)}) collective-permute-start(f32[1,128]{1,0:T(1,128)S(1)} %collective-permute-done.6), channel_id=1, source_target_pairs={{0,4},{4,8},{8,12},{12,16},{16,20},{20,24},{24,28},{28,0},{1,5},{5... | collective-permute-start | bytes 1544 | tf_op jit(solution)/shard_map/ppermute | solution.py:21
  139.3 6.2 %collective-permute-start.8 = (f32[1,128]{1,0:T(1,128)S(1)}, f32[1,128]{1,0:T(1,128)S(1)}, u32[]{:S(2)}, u32[]{:S(2)}) collective-permute-start(f32[1,128]{1,0:T(1,128)S(1)} %collective-permute-done.7), channel_id=1, source_target_pairs={{0,4},{4,8},{8,12},{12,16},{16,20},{20,24},{24,28},{28,0},{1,5},{5... | collective-permute-start | bytes 1544 | tf_op jit(solution)/shard_map/ppermute | solution.py:21
Sparse Core Ops, SparseCore 0:
  18.9 80.3 all-reduce.2
